TPU v7x, 512 devices: a whole 4x8x8 slice. The times are simulated.
512 devices in a mesh: expert: 128 (over z, y, core), tensor: 4 (over x).
Axes of the slice: x: 4, y: 8, z: 8, core: 2. Of those that a mesh axis runs over, the one named last changes fastest.
Arguments:
- attn_partial: bfloat16 [4, 4096, 3584], P('tensor', 'expert'), may hold values from -4 to 4
- residual_in: bfloat16 [4096, 3584], P(('expert', 'tensor')), may hold values from -6 to 6
- norm_gain: bfloat16 [3584], replicated, may hold values from 0.25 to 1.75
- w_in: bfloat16 [128, 3584, 1024], P('expert', None, 'tensor'), may hold values from -0.09375 to 0.09375
- w_out: bfloat16 [128, 1024, 3584], P('expert', 'tensor'), may hold values from -0.375 to 0.375
- routes: int32 [4096, 8], P('expert'), may hold values from 0 to 127, all different within a row; in each aligned block of 32 rows (0 to 31, 32 to 63, ...) at most 4 rows name the same one
- gate_weights: float32 [4096, 8], P('expert'), may hold values from 0.05 to 0.5
Outputs:
- layer_out: bfloat16 [4096, 3584], P('expert')
Inputs may be any that keep to these rules, and one draw needn't show every extreme that they name: `routes`: each row names 8 different experts. In each aligned block of 32 rows (the tokens of one index of expert) no expert is named by more than 4 rows, and in some block an expert is named by exactly 4 rows.
All inputs are finite; a program needn't handle non-finite values.
Results may differ from a plain program's by a relative error of at most 0.02.
Values may be sent and summed in bfloat16 or wider, within the bound.
No kernel may reach another device: no remote copies, remote signals or barrier semaphores. Data moves between devices by JAX's collectives and lax.ppermute only.
A program may use at most 64 MiB of HBM per device.

v0:
```python
import jax
import jax.numpy as jnp
from jax import lax
from jax.sharding import PartitionSpec as P

QB = 128
EPSILON = 1e-06


def capacity(group_tokens, top_count, expert_count):
    return min(group_tokens, max(4, 2 * group_tokens * top_count // expert_count))


def shards(attn_partial, residual_in, norm_gain, w_in, w_out, routes, gate_weights):
    group_tokens, top_count = routes.shape
    model_width = residual_in.shape[1]
    expert_count = lax.axis_size("expert")
    tensor_count = lax.axis_size("tensor")
    slot_count = capacity(group_tokens, top_count, expert_count)
    block_count = model_width // QB
    w_in_d = lax.all_to_all(w_in[0], "tensor", split_axis=0, concat_axis=1, tiled=True)
    w_out_d = lax.all_to_all(w_out[0], "tensor", split_axis=1, concat_axis=0, tiled=True)
    hidden_count = w_in_d.shape[1]
    hidden_quarter = hidden_count // tensor_count
    attention = lax.psum_scatter(
        attn_partial[0].astype(jnp.float32).astype(jnp.bfloat16),
        "tensor",
        scatter_dimension=0,
        tiled=True,
    ).astype(jnp.float32)
    residual = (residual_in.astype(jnp.float32) + attention).astype(jnp.bfloat16)
    stream = residual.astype(jnp.float32)
    rms_value = jnp.sqrt(jnp.mean(stream * stream, axis=1, keepdims=True) + EPSILON)
    normed = stream / rms_value * norm_gain.astype(jnp.float32)
    blocks = normed.reshape(-1, block_count, QB)
    block_scale = (jnp.max(jnp.abs(blocks), axis=2) + EPSILON).astype(jnp.bfloat16)
    scale_wide = block_scale.astype(jnp.float32)[:, :, None]
    quantized = (blocks / scale_wide).astype(jnp.bfloat16)
    expert_input = (
        (quantized.astype(jnp.float32) * scale_wide).reshape(-1, model_width).astype(jnp.bfloat16)
    )
    both = lax.all_to_all(
        jnp.stack([expert_input, residual]), "tensor", split_axis=2, concat_axis=1, tiled=True
    )
    group_input, group_resid = (both[0], both[1])
    pair_expert = routes.reshape(-1)
    onehot = (pair_expert[:, None] == jnp.arange(expert_count, dtype=jnp.int32)[None, :]).astype(
        jnp.int32
    )
    earlier = jnp.cumsum(onehot, axis=0) - onehot
    slot_index = jnp.sum(earlier * onehot, axis=1)
    target = pair_expert * slot_count + slot_index
    pair_total = group_tokens * top_count
    slot_table = (
        jnp.full((expert_count * slot_count,), -1, jnp.int32)
        .at[target]
        .set(jnp.arange(pair_total, dtype=jnp.int32))
    )
    slot_table = slot_table.reshape(expert_count, slot_count)
    filled = slot_table >= 0
    token_ids = jnp.maximum(slot_table, 0) // top_count
    row_block = jnp.where(filled[:, :, None], group_input[token_ids], jnp.zeros((), jnp.bfloat16))
    recv_rows = lax.all_to_all(row_block, "expert", split_axis=0, concat_axis=0, tiled=True)
    sources = recv_rows.shape[0]
    quarter = recv_rows.shape[2]
    rows = recv_rows.reshape(sources * slot_count, quarter)
    pre_partial = jnp.dot(rows, w_in_d, preferred_element_type=jnp.float32)
    pre_value = lax.psum_scatter(pre_partial, "tensor", scatter_dimension=1, tiled=True)
    hidden_part = jax.nn.silu(pre_value).astype(jnp.bfloat16)
    hidden = lax.all_gather(hidden_part, "tensor", axis=1, tiled=True)
    summed = jnp.zeros((rows.shape[0], quarter), jnp.float32)
    for lane in range(tensor_count):
        lo = lane * hidden_quarter
        term = jnp.dot(
            hidden[:, lo : lo + hidden_quarter],
            w_out_d[lo : lo + hidden_quarter],
            preferred_element_type=jnp.float32,
        ).astype(jnp.bfloat16)
        summed = summed + term.astype(jnp.float32)
    expert_out = summed.astype(jnp.bfloat16).reshape(sources, slot_count, quarter)
    returned = lax.all_to_all(expert_out, "expert", split_axis=0, concat_axis=0, tiled=True)
    flat_back = returned.reshape(expert_count * slot_count, quarter)
    picked = flat_back[target].astype(jnp.float32) * gate_weights.reshape(-1)[:, None]
    mixture = jnp.sum(picked.reshape(group_tokens, top_count, quarter), axis=1)
    out_part = (group_resid.astype(jnp.float32) + mixture).astype(jnp.bfloat16)
    return lax.all_gather(out_part, "tensor", axis=1, tiled=True)


def solution(mesh):
    return jax.shard_map(
        shards,
        mesh=mesh,
        in_specs=(
            P("tensor", "expert", None),
            P(("expert", "tensor"), None),
            P(),
            P("expert", None, "tensor"),
            P("expert", "tensor", None),
            P("expert", None),
            P("expert", None),
        ),
        out_specs=P("expert", None),
        check_vma=False,
    )
```

profile of v0, /device:TPU:10, one launch (start us, length us, event | category | flops | bytes accessed | tf_op | source)
XLA Modules:
  0.0 264.9 jit_solution(16002327998737600328)
XLA Ops:
  7.3 0.8 copy.47
  10.2 28.8 %reduce-scatter.3.cloned.1.call-done = bf16[8,3584]{1,0:T(8,128)(2,1)} async-done(((bf16[32,3584]{1,0:T(8,128)(2,1)}), bf16[8,3584]{1,0:T(8,128)(2,1)}) %reduce-scatter.3.cloned.1.call-update) | async-done | bytes 57360 | tf_op jit(solution)/shard_map/reduce_scatter | solution.py:25
  39.0 1.0 fusion.9
  40.3 2.5 copy.44
  42.8 2.6 reshape.198
  45.4 5.7 %all-to-all-start = ((bf16[4,2,7168]{2,1,0:T(2,128)(2,1)}), bf16[4,2,7168]{2,1,0:T(2,128)(2,1)S(1)}, u32[]{:S(2)}, u32[]{:S(2)}) async-start(bf16[4,2,7168]{2,1,0:T(2,128)(2,1)} %reshape.198), calls=%async_computation.1 | async-start | bytes 229376 | tf_op jit(solution)/shard_map/all_to_all | solution.py:42
  51.3 4.3 %all-to-all-done = bf16[4,2,7168]{2,1,0:T(2,128)(2,1)S(1)} async-done(((bf16[4,2,7168]{2,1,0:T(2,128)(2,1)}), bf16[4,2,7168]{2,1,0:T(2,128)(2,1)S(1)}, u32[]{:S(2)}, u32[]{:S(2)}) %all-to-all-start) | async-done | bytes 114720 | tf_op jit(solution)/shard_map/all_to_all | solution.py:42
  55.6 5.0 %all-to-all-start.2 = ((bf16[4,896,256]{2,1,0:T(8,128)(2,1)}), bf16[4,896,256]{2,1,0:T(8,128)(2,1)S(1)}, u32[]{:S(2)}, u32[]{:S(2)}) async-start(bf16[4,896,256]{2,1,0:T(8,128)(2,1)} %bitcast.79), calls=%async_computation.3 | async-start | bytes 3670016 | tf_op jit(solution)/shard_map/all_to_all | solution.py:21
  60.6 1.4 scatter_custom_fusion
  62.5 3.4 %reshape.199 = bf16[3584,2,8]{2,1,0:T(2,128)(2,1)} reshape(bf16[4,2,7168]{2,1,0:T(2,128)(2,1)S(1)} %all-to-all-done) | data formatting | bytes 229376
  65.9 4.3 %copy.45 = bf16[2,8,4,896]{3,1,2,0:T(8,128)(2,1)S(1)} copy(bf16[2,8,4,896]{1,0,3,2:T(2,128)(2,1)} %bitcast.78) | data formatting | bytes 229376 | tf_op jit(solution)/shard_map/all_to_all | solution.py:42
  70.3 2.8 %gather_fusion = bf16[512,896]{1,0:T(8,128)(2,1)} fusion(bf16[32,896]{1,0:T(8,128)(2,1)S(1)} %slice_bitcast_fusion.8, s32[1024]{0:T(1024)S(1)} %pad_clamp_fusion.1), kind=kCustom, calls=%fused_computation | custom fusion | bytes 1837056 | tf_op jit(solution)/shard_map/gather | solution.py:62
  73.0 1.8 reshape.172
  74.8 1.5 broadcast_select_fusion
  76.3 3.2 %all-to-all-done.2 = bf16[4,896,256]{2,1,0:T(8,128)(2,1)S(1)} async-done(((bf16[4,896,256]{2,1,0:T(8,128)(2,1)}), bf16[4,896,256]{2,1,0:T(8,128)(2,1)S(1)}, u32[]{:S(2)}, u32[]{:S(2)}) %all-to-all-start.2) | async-done | bytes 1835040 | tf_op jit(solution)/shard_map/all_to_all | solution.py:21
  79.5 14.2 %all-to-all-start.1 = ((bf16[128,4,896]{2,1,0:T(4,128)(2,1)}), bf16[128,4,896]{2,1,0:T(4,128)(2,1)S(1)}, u32[]{:S(2)}, u32[]{:S(2)}) async-start(bf16[128,4,896]{2,1,0:T(4,128)(2,1)} %broadcast_select_fusion), calls=%async_computation.2 | async-start | bytes 1835008 | tf_op jit(solution)/shard_map/all_to_all | solution.py:63
  93.7 2.4 copy.51
  96.2 26.1 %all-to-all-done.1 = bf16[128,4,896]{2,1,0:T(4,128)(2,1)S(1)} async-done(((bf16[128,4,896]{2,1,0:T(4,128)(2,1)}), bf16[128,4,896]{2,1,0:T(4,128)(2,1)S(1)}, u32[]{:S(2)}, u32[]{:S(2)}) %all-to-all-start.1) | async-done | bytes 917536 | tf_op jit(solution)/shard_map/all_to_all | solution.py:63
  122.2 1.1 reshape.166
  123.4 3.8 %fusion.20 = f32[512,1024]{1,0:T(8,128)} fusion(bf16[512,896]{1,0:T(8,128)(2,1)} %reshape.166, bf16[896,1024]{0,1:T(8,128)(2,1)S(1)} %bitcast.80), kind=kOutput, calls=%fused_computation.62 | convolution fusion | flops 939524096 | bytes 4849664 | tf_op jit(solution)/shard_map/dot_general | solution.py:67
  127.4 25.9 %reduce-scatter.5.cloned.1.call-done = f32[512,256]{1,0:T(8,128)} async-done(((f32[512,1024]{1,0:T(8,128)}), f32[512,256]{1,0:T(8,128)}) %reduce-scatter.5.cloned.1.call-update) | async-done | bytes 524304 | tf_op jit(solution)/shard_map/reduce_scatter | solution.py:68
  153.3 1.9 multiply_convert_fusion
  155.3 2.3 copy.52
  157.6 33.2 %all_to_all.60 = bf16[256,4,896]{0,2,1:T(8,128)(2,1)S(1)} all-to-all(bf16[256,4,896]{0,2,1:T(8,128)(2,1)} %bitcast.76), channel_id=1, replica_groups=mesh['expert'=128,'tensor'=4] {'tensor'}, dimensions={1} | all-to-all | bytes 3670016 | tf_op jit(solution)/shard_map/all_to_all | solution.py:22
  190.8 5.0 %all-gather.2.cloned.1.call-done = bf16[512,1024]{1,0:T(8,128)(2,1)} async-done(((bf16[512,256]{1,0:T(8,128)(2,1)}), bf16[512,1024]{1,0:T(8,128)(2,1)}) %all-gather.2.cloned.1.call-update) | async-done | bytes 1048592 | tf_op jit(solution)/shard_map/all_gather | solution.py:70
  195.8 1.5 convolution_convert_fusion.2
  197.3 1.4 convolution_convert_fusion.1
  199.8 1.1 reshape.167
  201.0 14.2 %all-to-all-start.4 = ((bf16[128,4,896]{2,1,0:T(4,128)(2,1)}), bf16[128,4,896]{2,1,0:T(4,128)(2,1)S(1)}, u32[]{:S(2)}, u32[]{:S(2)}) async-start(bf16[128,4,896]{2,1,0:T(4,128)(2,1)} %reshape.167), calls=%async_computation.6 | async-start | bytes 1835008 | tf_op jit(solution)/shard_map/all_to_all | solution.py:81
  215.2 28.5 %all-to-all-done.4 = bf16[128,4,896]{2,1,0:T(4,128)(2,1)S(1)} async-done(((bf16[128,4,896]{2,1,0:T(4,128)(2,1)}), bf16[128,4,896]{2,1,0:T(4,128)(2,1)S(1)}, u32[]{:S(2)}, u32[]{:S(2)}) %all-to-all-start.4) | async-done | bytes 917536 | tf_op jit(solution)/shard_map/all_to_all | solution.py:81
  243.9 1.2 gather_fusion.1
  245.5 12.2 %all_gather.7 = bf16[32,3584]{1,0:T(8,128)(2,1)S(1)} all-gather(bf16[32,896]{1,0:T(8,128)(2,1)S(1)} %fusion.13), channel_id=1, replica_groups=mesh['expert'=128,'tensor'=4] {'tensor'}, dimensions={1}, use_global_device_ids=true | all-gather | bytes 286720 | tf_op jit(solution)/shard_map/all_gather | solution.py:86
  (53 shorter events, 6.6 us)
Async XLA Ops:
  6.5 32.4 %reduce-scatter.3.cloned.1.call-start = ((), (), s32[]{:S(2)}) async-start(), calls=%async_computation.7 | async-start | bytes 286720 | tf_op jit(solution)/shard_map/reduce_scatter | solution.py:25
  45.4 10.1 %all-to-all-start = ((bf16[4,2,7168]{2,1,0:T(2,128)(2,1)}), bf16[4,2,7168]{2,1,0:T(2,128)(2,1)S(1)}, u32[]{:S(2)}, u32[]{:S(2)}) async-start(bf16[4,2,7168]{2,1,0:T(2,128)(2,1)} %reshape.198), calls=%async_computation.1 | async-start | bytes 229376 | tf_op jit(solution)/shard_map/all_to_all | solution.py:42
  55.6 23.9 %all-to-all-start.2 = ((bf16[4,896,256]{2,1,0:T(8,128)(2,1)}), bf16[4,896,256]{2,1,0:T(8,128)(2,1)S(1)}, u32[]{:S(2)}, u32[]{:S(2)}) async-start(bf16[4,896,256]{2,1,0:T(8,128)(2,1)} %bitcast.79), calls=%async_computation.3 | async-start | bytes 3670016 | tf_op jit(solution)/shard_map/all_to_all | solution.py:21
  79.5 42.7 %all-to-all-start.1 = ((bf16[128,4,896]{2,1,0:T(4,128)(2,1)}), bf16[128,4,896]{2,1,0:T(4,128)(2,1)S(1)}, u32[]{:S(2)}, u32[]{:S(2)}) async-start(bf16[128,4,896]{2,1,0:T(4,128)(2,1)} %broadcast_select_fusion), calls=%async_computation.2 | async-start | bytes 1835008 | tf_op jit(solution)/shard_map/all_to_all | solution.py:63
  93.7 59.7 %reduce-scatter.5.cloned.1.call-start = ((), (), s32[]{:S(2)}) async-start(), calls=%async_computation.8 | async-start | bytes 2621440 | tf_op jit(solution)/shard_map/reduce_scatter | solution.py:68
  96.2 27.2 %copy-start.1 = (bf16[896,4,256]{0,2,1:T(8,128)(2,1)S(1)}, bf16[896,4,256]{0,2,1:T(8,128)(2,1)}, u32[]{:S(2)}) copy-start(bf16[896,4,256]{0,2,1:T(8,128)(2,1)} %copy.51) | copy-start | bytes 5505028
  127.2 28.1 %copy-start = (bf16[1,256,3584]{2,1,0:T(8,128)(2,1)S(1)}, bf16[1,256,3584]{2,1,0:T(8,128)(2,1)}, u32[]{:S(2)}) copy-start(bf16[1,256,3584]{2,1,0:T(8,128)(2,1)} %param.11) | copy-start | bytes 5505028
  127.2 68.6 %all-gather.2.cloned.1.call-start = ((), (), s32[]{:S(2)}) async-start(), calls=%async_computation.9 | async-start | bytes 1310720 | tf_op jit(solution)/shard_map/all_gather | solution.py:70
  195.8 2.9 %copy-start.2 = (bf16[512,1024]{1,0:T(8,128)(2,1)S(1)}, bf16[512,1024]{1,0:T(8,128)(2,1)}, u32[]{:S(2)}) copy-start(bf16[512,1024]{1,0:T(8,128)(2,1)} %all-gather.2.cloned.1.call-done) | copy-start | bytes 3145732
  199.8 15.3 %copy-start.3 = (f32[32,8]{0,1:T(8,128)S(1)}, f32[32,8]{0,1:T(8,128)}, u32[]{:S(2)}) copy-start(f32[32,8]{0,1:T(8,128)} %param.13) | copy-start | bytes 3076
  201.0 42.7 %all-to-all-start.4 = ((bf16[128,4,896]{2,1,0:T(4,128)(2,1)}), bf16[128,4,896]{2,1,0:T(4,128)(2,1)S(1)}, u32[]{:S(2)}, u32[]{:S(2)}) async-start(bf16[128,4,896]{2,1,0:T(4,128)(2,1)} %reshape.167), calls=%async_computation.6 | async-start | bytes 1835008 | tf_op jit(solution)/shard_map/all_to_all | solution.py:81
Sparse Core Ops, SparseCore 0:
  10.1 28.8 reduce-scatter.2
  127.3 25.9 reduce-scatter.4
  155.4 40.2 all-gather.1
where the time goes:
time: 266 us; the launch traced here: 265 us
  waiting for transfers between devices  122 us (46%)
  blocking collectives  45.5 us (17%)
  starting transfers between devices  39.3 us (15%)
  local copies, waits for them, and re-layouts  29.7 us (11%)
  between operations  13.4 us (5%)
  matrix products  7.82 us (3%)
  other arithmetic  6.91 us (3%)
    all_to_all x1, blocking collectives, shards(): lax.all_to_all(w_out[0], 'tensor', split_axis=1, concat_axis=0, tiled=True)  33.2 us
    reduce_scatter x1, waiting for transfers between devices, shards(): lax.psum_scatter(attn_partial[0].astype(jnp.float32).astype(jnp.bfloat16)...  28.8 us
    all_to_all x1, waiting for transfers between devices, shards(): lax.all_to_all(expert_out, 'expert', split_axis=0, concat_axis=0, tiled=T...  28.5 us
    all_to_all x1, waiting for transfers between devices, shards(): lax.all_to_all(row_block, 'expert', split_axis=0, concat_axis=0, tiled=True)  26.1 us
    reduce_scatter x1, waiting for transfers between devices, shards(): lax.psum_scatter(pre_partial, 'tensor', scatter_dimension=1, tiled=True)  25.9 us
    all_to_all x1, starting transfers between devices, shards(): lax.all_to_all(row_block, 'expert', split_axis=0, concat_axis=0, tiled=True)  14.2 us
    all_to_all x1, starting transfers between devices, shards(): lax.all_to_all(expert_out, 'expert', split_axis=0, concat_axis=0, tiled=T...  14.2 us
    all_gather x1, blocking collectives, shards(): return lax.all_gather(out_part, 'tensor', axis=1, tiled=True)  12.2 us
  transfers between devices with their start and end apart: 7, of which 7 were waited for; matrix products, arithmetic and copies ran while one was open for 9% of the time, Pallas kernels for 0%

commit v1 on v0

--- a/solution.py
+++ b/solution.py
@@ -5,6 +5,19 @@
 
 QB = 128
 EPSILON = 1e-06
+
+
+def ring_gather(x, axis, dim):
+    ways = lax.axis_size(axis)
+    up = [(d, (d + 1) % ways) for d in range(ways)]
+    down = [(d, (d - 1) % ways) for d in range(ways)]
+    earlier, later = ([x], [x])
+    for _ in range(ways // 2):
+        earlier.append(lax.ppermute(earlier[-1], axis, up))
+    for _ in range((ways - 1) // 2):
+        later.append(lax.ppermute(later[-1], axis, down))
+    line = jnp.concatenate([*earlier[::-1], *later[1:]], axis=dim)
+    return jnp.roll(line, (lax.axis_index(axis) - ways // 2) * x.shape[dim], axis=dim)
 
 
 def capacity(group_tokens, top_count, expert_count):
@@ -83,7 +96,7 @@
     picked = flat_back[target].astype(jnp.float32) * gate_weights.reshape(-1)[:, None]
     mixture = jnp.sum(picked.reshape(group_tokens, top_count, quarter), axis=1)
     out_part = (group_resid.astype(jnp.float32) + mixture).astype(jnp.bfloat16)
-    return lax.all_gather(out_part, "tensor", axis=1, tiled=True)
+    return ring_gather(out_part, "tensor", 1)
 
 
 def solution(mesh):

time: 266 us -> 271 us (1.019)
  the two profiles are of different devices: /device:TPU:10 before, /device:TPU:14 now
where the time goes in v1:
time: 271 us; the launch traced here: 270 us
  waiting for transfers between devices  130 us (48%)
  starting transfers between devices  48 us (18%)
  blocking collectives  33.2 us (12%)
  local copies, waits for them, and re-layouts  29.9 us (11%)
  between operations  13.4 us (5%)
  matrix products  7.81 us (3%)
  other arithmetic  6.93 us (3%)
    all_to_all x1, blocking collectives, shards(): lax.all_to_all(w_out[0], 'tensor', split_axis=1, concat_axis=0, tiled=True)  33.2 us
    reduce_scatter x1, waiting for transfers between devices, shards(): lax.psum_scatter(attn_partial[0].astype(jnp.float32).astype(jnp.bfloat16)...  28.7 us
    all_to_all x1, waiting for transfers between devices, shards(): lax.all_to_all(expert_out, 'expert', split_axis=0, concat_axis=0, tiled=T...  28.5 us
    all_to_all x1, waiting for transfers between devices, shards(): lax.all_to_all(row_block, 'expert', split_axis=0, concat_axis=0, tiled=True)  26.1 us
    reduce_scatter x1, waiting for transfers between devices, shards(): lax.psum_scatter(pre_partial, 'tensor', scatter_dimension=1, tiled=True)  25.9 us
    all_to_all x1, starting transfers between devices, shards(): lax.all_to_all(expert_out, 'expert', split_axis=0, concat_axis=0, tiled=T...  14.2 us
    all_to_all x1, starting transfers between devices, shards(): lax.all_to_all(row_block, 'expert', split_axis=0, concat_axis=0, tiled=True)  14.2 us
    unnamed x21, local copies, waits for them, and re-layouts  9.27 us
  transfers between devices with their start and end apart: 10, of which 10 were waited for; matrix products, arithmetic and copies ran while one was open for 9% of the time, Pallas kernels for 0%

profile of v1, /device:TPU:14, one launch (start us, length us, event | category | flops | bytes accessed | tf_op | source)
XLA Modules:
  0.0 269.7 jit_solution(11239441242730784967)
XLA Ops:
  10.2 28.7 %reduce-scatter.3.cloned.1.call-done = bf16[8,3584]{1,0:T(8,128)(2,1)} async-done(((bf16[32,3584]{1,0:T(8,128)(2,1)}), bf16[8,3584]{1,0:T(8,128)(2,1)}) %reduce-scatter.3.cloned.1.call-update) | async-done | bytes 57360 | tf_op jit(solution)/shard_map/reduce_scatter | solution.py:38
  40.3 2.5 copy.44
  42.8 2.6 reshape.198
  45.4 5.7 %all-to-all-start = ((bf16[4,2,7168]{2,1,0:T(2,128)(2,1)}), bf16[4,2,7168]{2,1,0:T(2,128)(2,1)S(1)}, u32[]{:S(2)}, u32[]{:S(2)}) async-start(bf16[4,2,7168]{2,1,0:T(2,128)(2,1)} %reshape.198), calls=%async_computation.1 | async-start | bytes 229376 | tf_op jit(solution)/shard_map/all_to_all | solution.py:55
  51.3 3.6 %all-to-all-done = bf16[4,2,7168]{2,1,0:T(2,128)(2,1)S(1)} async-done(((bf16[4,2,7168]{2,1,0:T(2,128)(2,1)}), bf16[4,2,7168]{2,1,0:T(2,128)(2,1)S(1)}, u32[]{:S(2)}, u32[]{:S(2)}) %all-to-all-start) | async-done | bytes 114720 | tf_op jit(solution)/shard_map/all_to_all | solution.py:55
  54.9 5.6 %all-to-all-start.2 = ((bf16[4,896,256]{2,1,0:T(8,128)(2,1)}), bf16[4,896,256]{2,1,0:T(8,128)(2,1)S(1)}, u32[]{:S(2)}, u32[]{:S(2)}) async-start(bf16[4,896,256]{2,1,0:T(8,128)(2,1)} %bitcast.79), calls=%async_computation.3 | async-start | bytes 3670016 | tf_op jit(solution)/shard_map/all_to_all | solution.py:34
  60.5 1.4 scatter_custom_fusion
  62.5 3.4 %reshape.199 = bf16[3584,2,8]{2,1,0:T(2,128)(2,1)} reshape(bf16[4,2,7168]{2,1,0:T(2,128)(2,1)S(1)} %all-to-all-done) | data formatting | bytes 229376
  65.9 4.3 %copy.45 = bf16[2,8,4,896]{3,1,2,0:T(8,128)(2,1)S(1)} copy(bf16[2,8,4,896]{1,0,3,2:T(2,128)(2,1)} %bitcast.78) | data formatting | bytes 229376 | tf_op jit(solution)/shard_map/all_to_all | solution.py:55
  70.2 2.8 %gather_fusion = bf16[512,896]{1,0:T(8,128)(2,1)} fusion(bf16[32,896]{1,0:T(8,128)(2,1)S(1)} %slice_bitcast_fusion.8, s32[1024]{0:T(1024)S(1)} %pad_clamp_fusion.1), kind=kCustom, calls=%fused_computation | custom fusion | bytes 1837056 | tf_op jit(solution)/shard_map/gather | solution.py:75
  73.0 1.8 reshape.172
  74.8 1.5 broadcast_select_fusion
  76.3 2.6 all-to-all-done.2
  78.8 14.2 %all-to-all-start.1 = ((bf16[128,4,896]{2,1,0:T(4,128)(2,1)}), bf16[128,4,896]{2,1,0:T(4,128)(2,1)S(1)}, u32[]{:S(2)}, u32[]{:S(2)}) async-start(bf16[128,4,896]{2,1,0:T(4,128)(2,1)} %broadcast_select_fusion), calls=%async_computation.2 | async-start | bytes 1835008 | tf_op jit(solution)/shard_map/all_to_all | solution.py:76
  93.0 2.4 copy.51
  95.5 26.1 %all-to-all-done.1 = bf16[128,4,896]{2,1,0:T(4,128)(2,1)S(1)} async-done(((bf16[128,4,896]{2,1,0:T(4,128)(2,1)}), bf16[128,4,896]{2,1,0:T(4,128)(2,1)S(1)}, u32[]{:S(2)}, u32[]{:S(2)}) %all-to-all-start.1) | async-done | bytes 917536 | tf_op jit(solution)/shard_map/all_to_all | solution.py:76
  122.7 3.8 %fusion.20 = f32[512,1024]{1,0:T(8,128)} fusion(bf16[512,896]{1,0:T(8,128)(2,1)} %reshape.166, bf16[896,1024]{0,1:T(8,128)(2,1)S(1)} %bitcast.80), kind=kOutput, calls=%fused_computation.71 | convolution fusion | flops 939524096 | bytes 4849664 | tf_op jit(solution)/shard_map/dot_general | solution.py:80
  126.8 25.9 %reduce-scatter.5.cloned.1.call-done = f32[512,256]{1,0:T(8,128)} async-done(((f32[512,1024]{1,0:T(8,128)}), f32[512,256]{1,0:T(8,128)}) %reduce-scatter.5.cloned.1.call-update) | async-done | bytes 524304 | tf_op jit(solution)/shard_map/reduce_scatter | solution.py:81
  152.7 1.9 multiply_convert_fusion
  154.6 2.3 copy.52
  156.9 33.2 %all_to_all.60 = bf16[256,4,896]{0,2,1:T(8,128)(2,1)S(1)} all-to-all(bf16[256,4,896]{0,2,1:T(8,128)(2,1)} %bitcast.76), channel_id=1, replica_groups=mesh['expert'=128,'tensor'=4] {'tensor'}, dimensions={1} | all-to-all | bytes 3670016 | tf_op jit(solution)/shard_map/all_to_all | solution.py:35
  190.2 5.5 %all-gather.2.cloned.1.call-done = bf16[512,1024]{1,0:T(8,128)(2,1)} async-done(((bf16[512,256]{1,0:T(8,128)(2,1)}), bf16[512,1024]{1,0:T(8,128)(2,1)}) %all-gather.2.cloned.1.call-update) | async-done | bytes 1048592 | tf_op jit(solution)/shard_map/all_gather | solution.py:83
  195.7 1.5 convolution_convert_fusion.2
  197.2 1.4 convolution_convert_fusion.1
  200.9 14.2 %all-to-all-start.4 = ((bf16[128,4,896]{2,1,0:T(4,128)(2,1)}), bf16[128,4,896]{2,1,0:T(4,128)(2,1)S(1)}, u32[]{:S(2)}, u32[]{:S(2)}) async-start(bf16[128,4,896]{2,1,0:T(4,128)(2,1)} %reshape.167), calls=%async_computation.6 | async-start | bytes 1835008 | tf_op jit(solution)/shard_map/all_to_all | solution.py:94
  215.2 28.5 %all-to-all-done.4 = bf16[128,4,896]{2,1,0:T(4,128)(2,1)S(1)} async-done(((bf16[128,4,896]{2,1,0:T(4,128)(2,1)}), bf16[128,4,896]{2,1,0:T(4,128)(2,1)S(1)}, u32[]{:S(2)}, u32[]{:S(2)}) %all-to-all-start.4) | async-done | bytes 917536 | tf_op jit(solution)/shard_map/all_to_all | solution.py:94
  243.8 1.2 gather_fusion.1
  245.4 2.2 collective-permute-start
  247.6 3.8 %collective-permute-done = bf16[32,896]{1,0:T(8,128)(2,1)S(1)} collective-permute-done((bf16[32,896]{1,0:T(8,128)(2,1)S(1)}, bf16[32,896]{1,0:T(8,128)(2,1)S(1)}, u32[]{:S(2)}, u32[]{:S(2)}) %collective-permute-start) | collective-permute-done | bytes 57376 | tf_op jit(solution)/shard_map/ppermute | solution.py:16
  251.5 3.4 %collective-permute-start.1 = (bf16[32,896]{1,0:T(8,128)(2,1)S(1)}, bf16[32,896]{1,0:T(8,128)(2,1)S(1)}, u32[]{:S(2)}, u32[]{:S(2)}) collective-permute-start(bf16[32,896]{1,0:T(8,128)(2,1)S(1)} %collective-permute-done), channel_id=1, source_target_pairs={{0,1},{1,2},{2,3},{3,0},{4,5},{5,6},{6,7},{7,4},{8,9},{9,10},{10,1... | collective-permute-start | bytes 172040 | tf_op jit(solution)/shard_map/ppermute | solution.py:16
  254.9 2.4 collective-permute-start.2
  257.6 4.6 %collective-permute-done.2 = bf16[32,896]{1,0:T(8,128)(2,1)S(1)} collective-permute-done((bf16[32,896]{1,0:T(8,128)(2,1)S(1)}, bf16[32,896]{1,0:T(8,128)(2,1)S(1)}, u32[]{:S(2)}, u32[]{:S(2)}) %collective-permute-start.2) | collective-permute-done | bytes 57376 | tf_op jit(solution)/shard_map/ppermute | solution.py:18
  (66 shorter events, 11.1 us)
Async XLA Ops:
  6.5 32.4 %reduce-scatter.3.cloned.1.call-start = ((), (), s32[]{:S(2)}) async-start(), calls=%async_computation.7 | async-start | bytes 286720 | tf_op jit(solution)/shard_map/reduce_scatter | solution.py:38
  45.4 9.5 %all-to-all-start = ((bf16[4,2,7168]{2,1,0:T(2,128)(2,1)}), bf16[4,2,7168]{2,1,0:T(2,128)(2,1)S(1)}, u32[]{:S(2)}, u32[]{:S(2)}) async-start(bf16[4,2,7168]{2,1,0:T(2,128)(2,1)} %reshape.198), calls=%async_computation.1 | async-start | bytes 229376 | tf_op jit(solution)/shard_map/all_to_all | solution.py:55
  54.9 23.9 %all-to-all-start.2 = ((bf16[4,896,256]{2,1,0:T(8,128)(2,1)}), bf16[4,896,256]{2,1,0:T(8,128)(2,1)S(1)}, u32[]{:S(2)}, u32[]{:S(2)}) async-start(bf16[4,896,256]{2,1,0:T(8,128)(2,1)} %bitcast.79), calls=%async_computation.3 | async-start | bytes 3670016 | tf_op jit(solution)/shard_map/all_to_all | solution.py:34
  78.8 42.7 %all-to-all-start.1 = ((bf16[128,4,896]{2,1,0:T(4,128)(2,1)}), bf16[128,4,896]{2,1,0:T(4,128)(2,1)S(1)}, u32[]{:S(2)}, u32[]{:S(2)}) async-start(bf16[128,4,896]{2,1,0:T(4,128)(2,1)} %broadcast_select_fusion), calls=%async_computation.2 | async-start | bytes 1835008 | tf_op jit(solution)/shard_map/all_to_all | solution.py:76
  93.0 59.7 %reduce-scatter.5.cloned.1.call-start = ((), (), s32[]{:S(2)}) async-start(), calls=%async_computation.8 | async-start | bytes 2621440 | tf_op jit(solution)/shard_map/reduce_scatter | solution.py:81
  95.5 27.2 %copy-start.1 = (bf16[896,4,256]{0,2,1:T(8,128)(2,1)S(1)}, bf16[896,4,256]{0,2,1:T(8,128)(2,1)}, u32[]{:S(2)}) copy-start(bf16[896,4,256]{0,2,1:T(8,128)(2,1)} %copy.51) | copy-start | bytes 5505028
  126.5 28.1 %copy-start = (bf16[1,256,3584]{2,1,0:T(8,128)(2,1)S(1)}, bf16[1,256,3584]{2,1,0:T(8,128)(2,1)}, u32[]{:S(2)}) copy-start(bf16[1,256,3584]{2,1,0:T(8,128)(2,1)} %param.11) | copy-start | bytes 5505028
  126.5 69.2 %all-gather.2.cloned.1.call-start = ((), (), s32[]{:S(2)}) async-start(), calls=%async_computation.9 | async-start | bytes 1310720 | tf_op jit(solution)/shard_map/all_gather | solution.py:83
  195.7 2.9 %copy-start.2 = (bf16[512,1024]{1,0:T(8,128)(2,1)S(1)}, bf16[512,1024]{1,0:T(8,128)(2,1)}, u32[]{:S(2)}) copy-start(bf16[512,1024]{1,0:T(8,128)(2,1)} %all-gather.2.cloned.1.call-done) | copy-start | bytes 3145732
  199.7 15.3 %copy-start.3 = (f32[32,8]{0,1:T(8,128)S(1)}, f32[32,8]{0,1:T(8,128)}, u32[]{:S(2)}) copy-start(f32[32,8]{0,1:T(8,128)} %param.13) | copy-start | bytes 3076
  200.9 42.7 %all-to-all-start.4 = ((bf16[128,4,896]{2,1,0:T(4,128)(2,1)}), bf16[128,4,896]{2,1,0:T(4,128)(2,1)S(1)}, u32[]{:S(2)}, u32[]{:S(2)}) async-start(bf16[128,4,896]{2,1,0:T(4,128)(2,1)} %reshape.167), calls=%async_computation.6 | async-start | bytes 1835008 | tf_op jit(solution)/shard_map/all_to_all | solution.py:94
  245.4 6.1 %collective-permute-start = (bf16[32,896]{1,0:T(8,128)(2,1)S(1)}, bf16[32,896]{1,0:T(8,128)(2,1)S(1)}, u32[]{:S(2)}, u32[]{:S(2)}) collective-permute-start(bf16[32,896]{1,0:T(8,128)(2,1)S(1)} %fusion.13), channel_id=1, source_target_pairs={{0,1},{1,2},{2,3},{3,0},{4,5},{5,6},{6,7},{7,4},{8,9},{9,10},{10,1... | collective-permute-start | bytes 172040 | tf_op jit(solution)/shard_map/ppermute | solution.py:16
  251.5 6.1 %collective-permute-start.1 = (bf16[32,896]{1,0:T(8,128)(2,1)S(1)}, bf16[32,896]{1,0:T(8,128)(2,1)S(1)}, u32[]{:S(2)}, u32[]{:S(2)}) collective-permute-start(bf16[32,896]{1,0:T(8,128)(2,1)S(1)} %collective-permute-done), channel_id=1, source_target_pairs={{0,1},{1,2},{2,3},{3,0},{4,5},{5,6},{6,7},{7,4},{8,9},{9,10},{10,1... | collective-permute-start | bytes 172040 | tf_op jit(solution)/shard_map/ppermute | solution.py:16
  254.9 7.3 %collective-permute-start.2 = (bf16[32,896]{1,0:T(8,128)(2,1)S(1)}, bf16[32,896]{1,0:T(8,128)(2,1)S(1)}, u32[]{:S(2)}, u32[]{:S(2)}) collective-permute-start(bf16[32,896]{1,0:T(8,128)(2,1)S(1)} %fusion.13), channel_id=1, source_target_pairs={{0,3},{1,0},{2,1},{3,2},{4,7},{5,4},{6,5},{7,6},{8,11},{9,8},{10,9... | collective-permute-start | bytes 172040 | tf_op jit(solution)/shard_map/ppermute | solution.py:18
Sparse Core Ops, SparseCore 0:
  10.1 28.7 reduce-scatter.2
  126.7 25.9 reduce-scatter.4
  154.8 40.8 all-gather.1
